TPU v7x, 32 devices: a whole 2x2x4 slice. The times are simulated.
32 devices in a mesh: grid: 8 (over z, y), band: 4 (over x, core).
Axes of the slice: x: 2, y: 2, z: 4, core: 2. Of those that a mesh axis runs over, the one named last changes fastest.
Arguments:
- orbitals: float32 [2048, 512], P('grid', 'band'), may hold values from -30 to 30
- potential: float32 [2048], P('grid'), may hold values from -1 to 1
- fitted: bfloat16 [512, 2048], P('band', 'grid'), may hold values from -6 to 6
- points: int32 [512], P('grid'), may hold values from -1 to 255, as said below
Outputs:
- updated: float32 [2048, 512], P('grid', 'band')
Inputs may be any that keep to these rules, and one draw needn't show every extreme that they name: Each block of 64 slots of one index of grid holds distinct grid points in its first slots and -1 in the rest; the numbers of filled slots of blocks 2i and 2i + 1 sum to 64, so that 256 slots are filled in all, and some block is full.
All inputs are finite; a program needn't handle non-finite values.
Results may differ from a plain program's by a relative error of at most 0.024.
Values may be sent and summed in bfloat16 or wider, within the bound.
No kernel may reach another device: no remote copies, remote signals or barrier semaphores. Data moves between devices by JAX's collectives and lax.ppermute only.
A program may use at most 64 MiB of HBM per device.

v0:
```python
import jax
import jax.numpy as jnp
from jax import lax
from jax.sharding import PartitionSpec as P

ITERS = 2


def body(orbitals, potential, fitted, points):
    rows = orbitals.shape[0]
    block_width = orbitals.shape[1]
    nbands = lax.axis_size("band")
    ngroups = lax.axis_size("grid")
    total_orbitals = block_width * nbands
    valid_mask = points >= 0
    safe_idx = jnp.where(valid_mask, points, 0)
    psi = orbitals
    for step in range(ITERS):
        orbital_block = psi.astype(jnp.bfloat16)
        selected_points = jnp.where(
            valid_mask[:, None], orbital_block[safe_idx], jnp.zeros((), jnp.bfloat16)
        )
        collocation_matrix = lax.all_gather(selected_points, "grid", axis=0, tiled=True)
        product = lax.dot_general(
            collocation_matrix,
            orbital_block,
            (((1,), (1,)), ((), ())),
            preferred_element_type=jnp.float32,
        )
        proj = lax.psum_scatter(
            (product / total_orbitals).astype(jnp.bfloat16), "band", scatter_dimension=0, tiled=True
        ).astype(jnp.float32)
        tile_blocks = (fitted.astype(jnp.float32) * proj).astype(jnp.bfloat16)
        orbitals_at_slots = lax.all_to_all(
            collocation_matrix, "band", split_axis=0, concat_axis=1, tiled=True
        )
        partial_value = lax.dot_general(
            tile_blocks,
            orbitals_at_slots,
            (((0,), (0,)), ((), ())),
            preferred_element_type=jnp.float32,
        )
        applied = lax.psum_scatter(
            partial_value.astype(jnp.bfloat16), "band", scatter_dimension=1, tiled=True
        ).astype(jnp.float32)
        fresh = psi - 0.25 * (potential[:, None] * psi - applied)
        squares = lax.psum(jnp.sum(fresh * fresh, axis=0), "grid")
        psi = fresh * lax.rsqrt(squares / (rows * ngroups) + 1e-06)
    return psi


def solution(mesh):
    in_specs = (P("grid", "band"), P("grid"), P("band", "grid"), P("grid"))
    out_specs = P("grid", "band")
    return jax.shard_map(body, mesh=mesh, in_specs=in_specs, out_specs=out_specs, check_vma=False)
```

profile of v0, /device:TPU:0, one launch (start us, length us, event | category | flops | bytes accessed | tf_op | source)
XLA Modules:
  0.0 209.6 jit_solution(11900437040815080563)
XLA Ops:
  6.5 0.0 copy-start.3
  6.5 0.0 reduce-scatter.9.cloned.1.call-start
  6.5 0.7 compare_select_fusion
  7.3 0.0 copy-done.3
  7.3 0.9 convert_element_type.41
  8.2 0.6 gather_fusion
  8.8 0.1 broadcast_select_fusion.1
  8.9 32.3 %all_gather.6 = bf16[512,128]{1,0:T(8,128)(2,1)S(1)} all-gather(bf16[64,128]{1,0:T(8,128)(2,1)S(1)} %broadcast_select_fusion.1), channel_id=1, replica_groups=mesh['grid'=8,'band'=4] {'grid'}, dimensions={0}, use_global_device_ids=true | all-gather | bytes 147456 | tf_op jit(solution)/shard_map/all_gather | solution.py:23
  41.2 0.9 fusion
  42.1 0.0 reduce-scatter.9.cloned.1.call-update
  42.2 0.0 reduce-scatter.13.cloned.1.call-start
  42.2 0.1 copy.7
  42.4 0.0 copy-start.1
  42.4 7.3 %all_to_all.38 = bf16[4,128,128]{1,2,0:T(8,128)(2,1)S(1)} all-to-all(bf16[4,128,128]{1,2,0:T(8,128)(2,1)S(1)} %copy.7), channel_id=1, replica_groups=mesh['grid'=8,'band'=4] {'band'}, dimensions={0} | all-to-all | bytes 262144 | tf_op jit(solution)/shard_map/all_to_all | solution.py:34
  49.7 13.6 %reduce-scatter.9.cloned.1.call-done = bf16[128,256]{1,0:T(8,128)(2,1)} async-done(((bf16[512,256]{1,0:T(8,128)(2,1)}), bf16[128,256]{1,0:T(8,128)(2,1)}) %reduce-scatter.9.cloned.1.call-update) | async-done | bytes 65552 | tf_op jit(solution)/shard_map/reduce_scatter | solution.py:30
  63.3 0.0 copy-done.1
  63.3 1.1 convolution_convert_fusion.1
  64.4 0.8 copy.9
  65.2 0.0 reduce-scatter.13.cloned.1.call-update
  65.2 0.0 copy-start
  65.3 0.0 reduce-scatter.11.cloned.1.call-start
  65.3 20.6 %reduce-scatter.13.cloned.1.call-done = bf16[128,256]{1,0:T(8,128)(2,1)} async-done(((bf16[512,256]{1,0:T(8,128)(2,1)}), bf16[128,256]{1,0:T(8,128)(2,1)}) %reduce-scatter.13.cloned.1.call-update) | async-done | bytes 65552
  85.9 0.0 copy-start.2
  85.9 1.0 copy.10
  86.9 0.0 copy-done
  86.9 0.0 copy-done.2
  86.9 0.1 multiply_reduce_fusion.1
  87.0 21.4 %psum.14 = f32[128]{0:T(128)S(1)} all-reduce(f32[128]{0:T(128)S(1)} %multiply_reduce_fusion.1), channel_id=1, replica_groups=mesh['grid'=8,'band'=4] {'grid'}, use_global_device_ids=true, to_apply=%region_3.4 | all-reduce | flops 128 | bytes 1024 | tf_op jit(solution)/shard_map/psum | solution.py:47
  108.4 0.1 multiply_convert_fusion
  108.5 0.6 gather_fusion.1
  109.2 0.1 broadcast_select_fusion
  109.3 30.5 %all_gather.7 = bf16[512,128]{1,0:T(8,128)(2,1)S(1)} all-gather(bf16[64,128]{1,0:T(8,128)(2,1)S(1)} %broadcast_select_fusion), channel_id=1, replica_groups=mesh['grid'=8,'band'=4] {'grid'}, dimensions={0}, use_global_device_ids=true | all-gather | bytes 147456 | tf_op jit(solution)/shard_map/all_gather | solution.py:23
  139.8 0.9 fusion.1
  140.7 0.0 reduce-scatter.11.cloned.1.call-update
  140.7 0.0 reduce-scatter.15.cloned.1.call-start
  140.8 0.1 copy.8
  140.9 7.0 %all_to_all.39 = bf16[4,128,128]{1,2,0:T(8,128)(2,1)S(1)} all-to-all(bf16[4,128,128]{1,2,0:T(8,128)(2,1)S(1)} %copy.8), channel_id=1, replica_groups=mesh['grid'=8,'band'=4] {'band'}, dimensions={0} | all-to-all | bytes 262144 | tf_op jit(solution)/shard_map/all_to_all | solution.py:34
  147.9 9.3 %reduce-scatter.11.cloned.1.call-done = bf16[128,256]{1,0:T(8,128)(2,1)} async-done(((bf16[512,256]{1,0:T(8,128)(2,1)}), bf16[128,256]{1,0:T(8,128)(2,1)}) %reduce-scatter.11.cloned.1.call-update) | async-done | bytes 65552 | tf_op jit(solution)/shard_map/reduce_scatter | solution.py:30
  157.3 1.1 convolution_convert_fusion
  158.3 0.8 copy.11
  159.2 0.0 reduce-scatter.15.cloned.1.call-update
  159.2 20.6 %reduce-scatter.15.cloned.1.call-done = bf16[128,256]{1,0:T(8,128)(2,1)} async-done(((bf16[512,256]{1,0:T(8,128)(2,1)}), bf16[128,256]{1,0:T(8,128)(2,1)}) %reduce-scatter.15.cloned.1.call-update) | async-done | bytes 65552
  179.8 0.9 copy.12
  180.7 0.1 multiply_reduce_fusion
  180.9 21.4 %psum.15 = f32[128]{0:T(128)S(1)} all-reduce(f32[128]{0:T(128)S(1)} %multiply_reduce_fusion), channel_id=1, replica_groups=mesh['grid'=8,'band'=4] {'grid'}, use_global_device_ids=true, to_apply=%region_7.8 | all-reduce | flops 128 | bytes 1024 | tf_op jit(solution)/shard_map/psum | solution.py:47
  202.3 0.8 broadcast_multiply_fusion
  (4 shorter events, 0.0 us)
Async XLA Ops:
  6.5 0.7 copy-start.3
  6.5 56.7 %reduce-scatter.9.cloned.1.call-start = ((), (), s32[]{:S(2)}) async-start(), calls=%async_computation.6 | async-start | bytes 327680 | tf_op jit(solution)/shard_map/reduce_scatter | solution.py:30
  42.2 43.8 %reduce-scatter.13.cloned.1.call-start = ((), (), s32[]{:S(2)}) async-start(), calls=%async_computation.8 | async-start | bytes 327680
  42.4 20.9 %copy-start.1 = (bf16[128,256]{1,0:T(8,128)(2,1)S(1)}, bf16[128,256]{1,0:T(8,128)(2,1)}, u32[]{:S(2)}) copy-start(bf16[128,256]{1,0:T(8,128)(2,1)} %param.6) | copy-start | bytes 196612
  65.2 21.7 %copy-start = (f32[256,128]{1,0:T(8,128)S(1)}, f32[256,128]{1,0:T(8,128)}, u32[]{:S(2)}) copy-start(f32[256,128]{1,0:T(8,128)} %param.4) | copy-start | bytes 393220
  65.3 92.0 %reduce-scatter.11.cloned.1.call-start = ((), (), s32[]{:S(2)}) async-start(), calls=%async_computation.7 | async-start | bytes 327680 | tf_op jit(solution)/shard_map/reduce_scatter | solution.py:30
  85.9 1.0 copy-start.2
  140.7 39.1 %reduce-scatter.15.cloned.1.call-start = ((), (), s32[]{:S(2)}) async-start(), calls=%async_computation.9 | async-start | bytes 327680
Sparse Core Ops, SparseCore 0:
  42.3 20.9 reduce-scatter.8
  65.9 19.9 reduce-scatter.12
  140.8 16.3 reduce-scatter.10
  159.7 20.0 reduce-scatter.14
where the time goes:
time: 210 us
  blocking collectives  120 us (57%)
  waiting for transfers between devices  64.2 us (31%)
  between operations  13.2 us (6%)
  local copies, waits for them, and re-layouts  5.13 us (2%)
  matrix products  4.03 us (2%)
  other arithmetic  2.98 us (1%)
    all_gather x2, blocking collectives, body(): lax.all_gather(selected_points, 'grid', axis=0, tiled=True)  62.8 us
    psum x2, blocking collectives, body(): squares = lax.psum(jnp.sum(fresh * fresh, axis=0), 'grid')  42.8 us
    unnamed x6, waiting for transfers between devices  41.3 us
    reduce_scatter x2, waiting for transfers between devices, body(): lax.psum_scatter((product / total_orbitals).astype(jnp.bfloat16), 'band',...  22.9 us
    all_to_all x2, blocking collectives, body(): lax.all_to_all(collocation_matrix, 'band', split_axis=0, concat_axis=1, t...  14.3 us
  transfers between devices with their start and end apart: 4, of which 4 were waited for; matrix products, arithmetic and copies ran while one was open for 0% of the time, Pallas kernels for 0%

commit v1 on v0

--- a/solution.py
+++ b/solution.py
@@ -20,7 +20,14 @@
         selected_points = jnp.where(
             valid_mask[:, None], orbital_block[safe_idx], jnp.zeros((), jnp.bfloat16)
         )
-        collocation_matrix = lax.all_gather(selected_points, "grid", axis=0, tiled=True)
+        ring = [selected_points]
+        for hop in range(7):
+            ring.append(lax.ppermute(ring[-1], "grid", [(dev, (dev + 1) % 8) for dev in range(8)]))
+        collocation_matrix = jnp.roll(
+            jnp.concatenate(ring[::-1], axis=0),
+            (lax.axis_index("grid") + 1) * ring[0].shape[0],
+            axis=0,
+        )
         product = lax.dot_general(
             collocation_matrix,
             orbital_block,

time: 210 us -> 236 us (1.12)
  waiting for transfers between devices: 64.2 us -> 149 us
  blocking collectives: 120 us -> 57.1 us
  starting transfers between devices: 0.13 us -> 3.17 us
    ppermute x0 -> x14, waiting for transfers between devices: none -> 88.4 us  [body(): lax.ppermute(ring[-1], 'grid', [(dev, (dev + 1) % 8) for dev in range(8)])]
    all_gather x2 -> x0, blocking collectives: 62.8 us -> none  [body(): lax.all_gather(selected_points, 'grid', axis=0, tiled=True)]
    reduce_scatter x2, waiting for transfers between devices: 22.9 us -> 19.4 us  [body(): lax.psum_scatter((product / total_orbitals).astype(jnp.bfloat16), 'band',...]
    ppermute x0 -> x14, starting transfers between devices: none -> 3.05 us  [body(): lax.ppermute(ring[-1], 'grid', [(dev, (dev + 1) % 8) for dev in range(8)])]
  transfers between devices with their start and end apart: 4 -> 18, of which waited for: 4 -> 18; matrix products, arithmetic and copies ran while one was open for 0% -> 0% of each run, Pallas kernels for 0% -> 0%
where the time goes in v1:
time: 236 us
  waiting for transfers between devices  149 us (63%)
  blocking collectives  57.1 us (24%)
  between operations  13.3 us (6%)
  local copies, waits for them, and re-layouts  5.25 us (2%)
  other arithmetic  4.09 us (2%)
  matrix products  4.04 us (2%)
  starting transfers between devices  3.17 us (1%)
    ppermute x14, waiting for transfers between devices, body(): lax.ppermute(ring[-1], 'grid', [(dev, (dev + 1) % 8) for dev in range(8)])  88.4 us
    psum x2, blocking collectives, body(): squares = lax.psum(jnp.sum(fresh * fresh, axis=0), 'grid')  42.7 us
    unnamed x6, waiting for transfers between devices  41.3 us
    reduce_scatter x2, waiting for transfers between devices, body(): lax.psum_scatter((product / total_orbitals).astype(jnp.bfloat16), 'band',...  19.4 us
    all_to_all x2, blocking collectives, body(): lax.all_to_all(collocation_matrix, 'band', split_axis=0, concat_axis=1, t...  14.4 us
  transfers between devices with their start and end apart: 18, of which 18 were waited for; matrix products, arithmetic and copies ran while one was open for 0% of the time, Pallas kernels for 0%

profile of v1, /device:TPU:0, one launch (start us, length us, event | category | flops | bytes accessed | tf_op | source)
XLA Modules:
  0.0 236.0 jit_solution(11330332474948943555)
XLA Ops:
  6.5 0.7 compare_select_fusion
  7.3 0.9 convert_element_type.41
  8.2 0.6 gather_fusion
  8.8 0.1 broadcast_select_fusion.1
  8.9 3.0 %collective-permute-start = (bf16[64,128]{1,0:T(8,128)(2,1)S(1)}, bf16[64,128]{1,0:T(8,128)(2,1)S(1)}, u32[]{:S(2)}, u32[]{:S(2)}) collective-permute-start(bf16[64,128]{1,0:T(8,128)(2,1)S(1)} %broadcast_select_fusion.1), channel_id=1, source_target_pairs={{0,4},{4,8},{8,12},{12,16},{16,20},{20,24},{24,28},{28,0},{1,5},{5... | collective-permute-start | bytes 49160 | tf_op jit(solution)/shard_map/ppermute | solution.py:25
  11.9 4.8 %collective-permute-done = bf16[64,128]{1,0:T(8,128)(2,1)S(1)} collective-permute-done((bf16[64,128]{1,0:T(8,128)(2,1)S(1)}, bf16[64,128]{1,0:T(8,128)(2,1)S(1)}, u32[]{:S(2)}, u32[]{:S(2)}) %collective-permute-start) | collective-permute-done | bytes 16416 | tf_op jit(solution)/shard_map/ppermute | solution.py:25
  16.7 6.4 %collective-permute-done.1 = bf16[64,128]{1,0:T(8,128)(2,1)S(1)} collective-permute-done((bf16[64,128]{1,0:T(8,128)(2,1)S(1)}, bf16[64,128]{1,0:T(8,128)(2,1)S(1)}, u32[]{:S(2)}, u32[]{:S(2)}) %collective-permute-start.1) | collective-permute-done | bytes 16416 | tf_op jit(solution)/shard_map/ppermute | solution.py:25
  23.1 6.4 %collective-permute-done.2 = bf16[64,128]{1,0:T(8,128)(2,1)S(1)} collective-permute-done((bf16[64,128]{1,0:T(8,128)(2,1)S(1)}, bf16[64,128]{1,0:T(8,128)(2,1)S(1)}, u32[]{:S(2)}, u32[]{:S(2)}) %collective-permute-start.2) | collective-permute-done | bytes 16416 | tf_op jit(solution)/shard_map/ppermute | solution.py:25
  29.5 6.4 %collective-permute-done.3 = bf16[64,128]{1,0:T(8,128)(2,1)S(1)} collective-permute-done((bf16[64,128]{1,0:T(8,128)(2,1)S(1)}, bf16[64,128]{1,0:T(8,128)(2,1)S(1)}, u32[]{:S(2)}, u32[]{:S(2)}) %collective-permute-start.3) | collective-permute-done | bytes 16416 | tf_op jit(solution)/shard_map/ppermute | solution.py:25
  36.0 6.4 %collective-permute-done.4 = bf16[64,128]{1,0:T(8,128)(2,1)S(1)} collective-permute-done((bf16[64,128]{1,0:T(8,128)(2,1)S(1)}, bf16[64,128]{1,0:T(8,128)(2,1)S(1)}, u32[]{:S(2)}, u32[]{:S(2)}) %collective-permute-start.4) | collective-permute-done | bytes 16416 | tf_op jit(solution)/shard_map/ppermute | solution.py:25
  42.4 6.4 %collective-permute-done.5 = bf16[64,128]{1,0:T(8,128)(2,1)S(1)} collective-permute-done((bf16[64,128]{1,0:T(8,128)(2,1)S(1)}, bf16[64,128]{1,0:T(8,128)(2,1)S(1)}, u32[]{:S(2)}, u32[]{:S(2)}) %collective-permute-start.5) | collective-permute-done | bytes 16416 | tf_op jit(solution)/shard_map/ppermute | solution.py:25
  48.9 6.4 %collective-permute-done.6 = bf16[64,128]{1,0:T(8,128)(2,1)S(1)} collective-permute-done((bf16[64,128]{1,0:T(8,128)(2,1)S(1)}, bf16[64,128]{1,0:T(8,128)(2,1)S(1)}, u32[]{:S(2)}, u32[]{:S(2)}) %collective-permute-start.6) | collective-permute-done | bytes 16416 | tf_op jit(solution)/shard_map/ppermute | solution.py:25
  55.4 0.1 constant_dynamic-update-slice_fusion
  55.4 0.5 fusion.5
  55.9 0.9 fusion
  56.9 0.0 reduce-scatter.13.cloned.1.call-start
  56.9 7.3 %all_to_all.38 = bf16[4,128,128]{2,1,0:T(8,128)(2,1)S(1)} all-to-all(bf16[4,128,128]{2,1,0:T(8,128)(2,1)S(1)} %bitcast.17), channel_id=1, replica_groups=mesh['grid'=8,'band'=4] {'band'}, dimensions={0} | all-to-all | bytes 262144 | tf_op jit(solution)/shard_map/all_to_all | solution.py:41
  64.3 0.1 copy.7
  64.4 10.1 %reduce-scatter.9.cloned.1.call-done = bf16[128,256]{1,0:T(8,128)(2,1)} async-done(((bf16[512,256]{1,0:T(8,128)(2,1)}), bf16[128,256]{1,0:T(8,128)(2,1)}) %reduce-scatter.9.cloned.1.call-update) | async-done | bytes 65552 | tf_op jit(solution)/shard_map/reduce_scatter | solution.py:37
  74.5 1.1 convolution_convert_fusion.1
  75.6 0.8 copy.9
  76.5 20.6 %reduce-scatter.13.cloned.1.call-done = bf16[128,256]{1,0:T(8,128)(2,1)} async-done(((bf16[512,256]{1,0:T(8,128)(2,1)}), bf16[128,256]{1,0:T(8,128)(2,1)}) %reduce-scatter.13.cloned.1.call-update) | async-done | bytes 65552
  97.2 1.0 copy.10
  98.2 0.1 multiply_reduce_fusion.1
  98.3 21.4 %psum.14 = f32[128]{0:T(128)S(1)} all-reduce(f32[128]{0:T(128)S(1)} %multiply_reduce_fusion.1), channel_id=1, replica_groups=mesh['grid'=8,'band'=4] {'grid'}, use_global_device_ids=true, to_apply=%region_3.5 | all-reduce | flops 128 | bytes 1024 | tf_op jit(solution)/shard_map/psum | solution.py:54
  119.6 0.1 multiply_convert_fusion
  119.8 0.6 gather_fusion.1
  120.4 0.1 broadcast_select_fusion
  120.5 6.4 %collective-permute-done.7 = bf16[64,128]{1,0:T(8,128)(2,1)S(1)} collective-permute-done((bf16[64,128]{1,0:T(8,128)(2,1)S(1)}, bf16[64,128]{1,0:T(8,128)(2,1)S(1)}, u32[]{:S(2)}, u32[]{:S(2)}) %collective-permute-start.7) | collective-permute-done | bytes 16416 | tf_op jit(solution)/shard_map/ppermute | solution.py:25
  126.9 6.4 %collective-permute-done.8 = bf16[64,128]{1,0:T(8,128)(2,1)S(1)} collective-permute-done((bf16[64,128]{1,0:T(8,128)(2,1)S(1)}, bf16[64,128]{1,0:T(8,128)(2,1)S(1)}, u32[]{:S(2)}, u32[]{:S(2)}) %collective-permute-start.8) | collective-permute-done | bytes 16416 | tf_op jit(solution)/shard_map/ppermute | solution.py:25
  133.4 6.4 %collective-permute-done.9 = bf16[64,128]{1,0:T(8,128)(2,1)S(1)} collective-permute-done((bf16[64,128]{1,0:T(8,128)(2,1)S(1)}, bf16[64,128]{1,0:T(8,128)(2,1)S(1)}, u32[]{:S(2)}, u32[]{:S(2)}) %collective-permute-start.9) | collective-permute-done | bytes 16416 | tf_op jit(solution)/shard_map/ppermute | solution.py:25
  139.8 6.4 %collective-permute-done.10 = bf16[64,128]{1,0:T(8,128)(2,1)S(1)} collective-permute-done((bf16[64,128]{1,0:T(8,128)(2,1)S(1)}, bf16[64,128]{1,0:T(8,128)(2,1)S(1)}, u32[]{:S(2)}, u32[]{:S(2)}) %collective-permute-start.10) | collective-permute-done | bytes 16416 | tf_op jit(solution)/shard_map/ppermute | solution.py:25
  146.2 6.4 %collective-permute-done.11 = bf16[64,128]{1,0:T(8,128)(2,1)S(1)} collective-permute-done((bf16[64,128]{1,0:T(8,128)(2,1)S(1)}, bf16[64,128]{1,0:T(8,128)(2,1)S(1)}, u32[]{:S(2)}, u32[]{:S(2)}) %collective-permute-start.11) | collective-permute-done | bytes 16416 | tf_op jit(solution)/shard_map/ppermute | solution.py:25
  152.7 6.4 %collective-permute-done.12 = bf16[64,128]{1,0:T(8,128)(2,1)S(1)} collective-permute-done((bf16[64,128]{1,0:T(8,128)(2,1)S(1)}, bf16[64,128]{1,0:T(8,128)(2,1)S(1)}, u32[]{:S(2)}, u32[]{:S(2)}) %collective-permute-start.12) | collective-permute-done | bytes 16416 | tf_op jit(solution)/shard_map/ppermute | solution.py:25
  159.1 6.4 %collective-permute-done.13 = bf16[64,128]{1,0:T(8,128)(2,1)S(1)} collective-permute-done((bf16[64,128]{1,0:T(8,128)(2,1)S(1)}, bf16[64,128]{1,0:T(8,128)(2,1)S(1)}, u32[]{:S(2)}, u32[]{:S(2)}) %collective-permute-start.13) | collective-permute-done | bytes 16416 | tf_op jit(solution)/shard_map/ppermute | solution.py:25
  165.6 0.1 constant_dynamic-update-slice_fusion.8
  165.7 0.5 fusion.4
  166.2 0.9 fusion.1
  167.2 7.0 %all_to_all.39 = bf16[4,128,128]{2,1,0:T(8,128)(2,1)S(1)} all-to-all(bf16[4,128,128]{2,1,0:T(8,128)(2,1)S(1)} %bitcast.16), channel_id=1, replica_groups=mesh['grid'=8,'band'=4] {'band'}, dimensions={0} | all-to-all | bytes 262144 | tf_op jit(solution)/shard_map/all_to_all | solution.py:41
  174.2 0.1 copy.8
  174.3 9.3 %reduce-scatter.11.cloned.1.call-done = bf16[128,256]{1,0:T(8,128)(2,1)} async-done(((bf16[512,256]{1,0:T(8,128)(2,1)}), bf16[128,256]{1,0:T(8,128)(2,1)}) %reduce-scatter.11.cloned.1.call-update) | async-done | bytes 65552 | tf_op jit(solution)/shard_map/reduce_scatter | solution.py:37
  183.7 1.1 convolution_convert_fusion
  184.8 0.8 copy.11
  185.6 20.6 %reduce-scatter.15.cloned.1.call-done = bf16[128,256]{1,0:T(8,128)(2,1)} async-done(((bf16[512,256]{1,0:T(8,128)(2,1)}), bf16[128,256]{1,0:T(8,128)(2,1)}) %reduce-scatter.15.cloned.1.call-update) | async-done | bytes 65552
  206.2 0.9 copy.12
  207.1 0.1 multiply_reduce_fusion
  207.3 21.4 %psum.15 = f32[128]{0:T(128)S(1)} all-reduce(f32[128]{0:T(128)S(1)} %multiply_reduce_fusion), channel_id=1, replica_groups=mesh['grid'=8,'band'=4] {'grid'}, use_global_device_ids=true, to_apply=%region_7.9 | all-reduce | flops 128 | bytes 1024 | tf_op jit(solution)/shard_map/psum | solution.py:54
  228.7 0.8 broadcast_multiply_fusion
  (46 shorter events, 0.4 us)
Async XLA Ops:
  6.5 0.7 copy-start.3
  6.5 68.0 %reduce-scatter.9.cloned.1.call-start = ((), (), s32[]{:S(2)}) async-start(), calls=%async_computation.6 | async-start | bytes 327680 | tf_op jit(solution)/shard_map/reduce_scatter | solution.py:37
  8.9 7.7 %collective-permute-start = (bf16[64,128]{1,0:T(8,128)(2,1)S(1)}, bf16[64,128]{1,0:T(8,128)(2,1)S(1)}, u32[]{:S(2)}, u32[]{:S(2)}) collective-permute-start(bf16[64,128]{1,0:T(8,128)(2,1)S(1)} %broadcast_select_fusion.1), channel_id=1, source_target_pairs={{0,4},{4,8},{8,12},{12,16},{16,20},{20,24},{24,28},{28,0},{1,5},{5... | collective-permute-start | bytes 49160 | tf_op jit(solution)/shard_map/ppermute | solution.py:25
  16.7 6.4 %collective-permute-start.1 = (bf16[64,128]{1,0:T(8,128)(2,1)S(1)}, bf16[64,128]{1,0:T(8,128)(2,1)S(1)}, u32[]{:S(2)}, u32[]{:S(2)}) collective-permute-start(bf16[64,128]{1,0:T(8,128)(2,1)S(1)} %collective-permute-done), channel_id=1, source_target_pairs={{0,4},{4,8},{8,12},{12,16},{16,20},{20,24},{24,28},{28,0},{1,5},{5... | collective-permute-start | bytes 49160 | tf_op jit(solution)/shard_map/ppermute | solution.py:25
  23.1 6.4 %collective-permute-start.2 = (bf16[64,128]{1,0:T(8,128)(2,1)S(1)}, bf16[64,128]{1,0:T(8,128)(2,1)S(1)}, u32[]{:S(2)}, u32[]{:S(2)}) collective-permute-start(bf16[64,128]{1,0:T(8,128)(2,1)S(1)} %collective-permute-done.1), channel_id=1, source_target_pairs={{0,4},{4,8},{8,12},{12,16},{16,20},{20,24},{24,28},{28,0},{1,5},{5... | collective-permute-start | bytes 49160 | tf_op jit(solution)/shard_map/ppermute | solution.py:25
  29.5 6.4 %collective-permute-start.3 = (bf16[64,128]{1,0:T(8,128)(2,1)S(1)}, bf16[64,128]{1,0:T(8,128)(2,1)S(1)}, u32[]{:S(2)}, u32[]{:S(2)}) collective-permute-start(bf16[64,128]{1,0:T(8,128)(2,1)S(1)} %collective-permute-done.2), channel_id=1, source_target_pairs={{0,4},{4,8},{8,12},{12,16},{16,20},{20,24},{24,28},{28,0},{1,5},{5... | collective-permute-start | bytes 49160 | tf_op jit(solution)/shard_map/ppermute | solution.py:25
  36.0 6.4 %collective-permute-start.4 = (bf16[64,128]{1,0:T(8,128)(2,1)S(1)}, bf16[64,128]{1,0:T(8,128)(2,1)S(1)}, u32[]{:S(2)}, u32[]{:S(2)}) collective-permute-start(bf16[64,128]{1,0:T(8,128)(2,1)S(1)} %collective-permute-done.3), channel_id=1, source_target_pairs={{0,4},{4,8},{8,12},{12,16},{16,20},{20,24},{24,28},{28,0},{1,5},{5... | collective-permute-start | bytes 49160 | tf_op jit(solution)/shard_map/ppermute | solution.py:25
  42.4 6.4 %collective-permute-start.5 = (bf16[64,128]{1,0:T(8,128)(2,1)S(1)}, bf16[64,128]{1,0:T(8,128)(2,1)S(1)}, u32[]{:S(2)}, u32[]{:S(2)}) collective-permute-start(bf16[64,128]{1,0:T(8,128)(2,1)S(1)} %collective-permute-done.4), channel_id=1, source_target_pairs={{0,4},{4,8},{8,12},{12,16},{16,20},{20,24},{24,28},{28,0},{1,5},{5... | collective-permute-start | bytes 49160 | tf_op jit(solution)/shard_map/ppermute | solution.py:25
  48.9 6.4 %collective-permute-start.6 = (bf16[64,128]{1,0:T(8,128)(2,1)S(1)}, bf16[64,128]{1,0:T(8,128)(2,1)S(1)}, u32[]{:S(2)}, u32[]{:S(2)}) collective-permute-start(bf16[64,128]{1,0:T(8,128)(2,1)S(1)} %collective-permute-done.5), channel_id=1, source_target_pairs={{0,4},{4,8},{8,12},{12,16},{16,20},{20,24},{24,28},{28,0},{1,5},{5... | collective-permute-start | bytes 49160 | tf_op jit(solution)/shard_map/ppermute | solution.py:25
  56.9 40.3 %reduce-scatter.13.cloned.1.call-start = ((), (), s32[]{:S(2)}) async-start(), calls=%async_computation.8 | async-start | bytes 327680
  64.3 10.2 %copy-start.1 = (bf16[128,256]{1,0:T(8,128)(2,1)S(1)}, bf16[128,256]{1,0:T(8,128)(2,1)}, u32[]{:S(2)}) copy-start(bf16[128,256]{1,0:T(8,128)(2,1)} %param.8) | copy-start | bytes 196612
  76.5 21.7 %copy-start = (f32[256,128]{1,0:T(8,128)S(1)}, f32[256,128]{1,0:T(8,128)}, u32[]{:S(2)}) copy-start(f32[256,128]{1,0:T(8,128)} %param.6) | copy-start | bytes 393220
  76.5 107.2 %reduce-scatter.11.cloned.1.call-start = ((), (), s32[]{:S(2)}) async-start(), calls=%async_computation.7 | async-start | bytes 327680 | tf_op jit(solution)/shard_map/reduce_scatter | solution.py:37
  97.2 1.0 copy-start.2
  120.5 6.5 %collective-permute-start.7 = (bf16[64,128]{1,0:T(8,128)(2,1)S(1)}, bf16[64,128]{1,0:T(8,128)(2,1)S(1)}, u32[]{:S(2)}, u32[]{:S(2)}) collective-permute-start(bf16[64,128]{1,0:T(8,128)(2,1)S(1)} %broadcast_select_fusion), channel_id=1, source_target_pairs={{0,4},{4,8},{8,12},{12,16},{16,20},{20,24},{24,28},{28,0},{1,5},{5... | collective-permute-start | bytes 49160 | tf_op jit(solution)/shard_map/ppermute | solution.py:25
  126.9 6.4 %collective-permute-start.8 = (bf16[64,128]{1,0:T(8,128)(2,1)S(1)}, bf16[64,128]{1,0:T(8,128)(2,1)S(1)}, u32[]{:S(2)}, u32[]{:S(2)}) collective-permute-start(bf16[64,128]{1,0:T(8,128)(2,1)S(1)} %collective-permute-done.7), channel_id=1, source_target_pairs={{0,4},{4,8},{8,12},{12,16},{16,20},{20,24},{24,28},{28,0},{1,5},{5... | collective-permute-start | bytes 49160 | tf_op jit(solution)/shard_map/ppermute | solution.py:25
  133.4 6.4 %collective-permute-start.9 = (bf16[64,128]{1,0:T(8,128)(2,1)S(1)}, bf16[64,128]{1,0:T(8,128)(2,1)S(1)}, u32[]{:S(2)}, u32[]{:S(2)}) collective-permute-start(bf16[64,128]{1,0:T(8,128)(2,1)S(1)} %collective-permute-done.8), channel_id=1, source_target_pairs={{0,4},{4,8},{8,12},{12,16},{16,20},{20,24},{24,28},{28,0},{1,5},{5... | collective-permute-start | bytes 49160 | tf_op jit(solution)/shard_map/ppermute | solution.py:25
  139.8 6.4 %collective-permute-start.10 = (bf16[64,128]{1,0:T(8,128)(2,1)S(1)}, bf16[64,128]{1,0:T(8,128)(2,1)S(1)}, u32[]{:S(2)}, u32[]{:S(2)}) collective-permute-start(bf16[64,128]{1,0:T(8,128)(2,1)S(1)} %collective-permute-done.9), channel_id=1, source_target_pairs={{0,4},{4,8},{8,12},{12,16},{16,20},{20,24},{24,28},{28,0},{1,5},{5... | collective-permute-start | bytes 49160 | tf_op jit(solution)/shard_map/ppermute | solution.py:25
  146.2 6.4 %collective-permute-start.11 = (bf16[64,128]{1,0:T(8,128)(2,1)S(1)}, bf16[64,128]{1,0:T(8,128)(2,1)S(1)}, u32[]{:S(2)}, u32[]{:S(2)}) collective-permute-start(bf16[64,128]{1,0:T(8,128)(2,1)S(1)} %collective-permute-done.10), channel_id=1, source_target_pairs={{0,4},{4,8},{8,12},{12,16},{16,20},{20,24},{24,28},{28,0},{1,5},{5... | collective-permute-start | bytes 49160 | tf_op jit(solution)/shard_map/ppermute | solution.py:25
  152.7 6.4 %collective-permute-start.12 = (bf16[64,128]{1,0:T(8,128)(2,1)S(1)}, bf16[64,128]{1,0:T(8,128)(2,1)S(1)}, u32[]{:S(2)}, u32[]{:S(2)}) collective-permute-start(bf16[64,128]{1,0:T(8,128)(2,1)S(1)} %collective-permute-done.11), channel_id=1, source_target_pairs={{0,4},{4,8},{8,12},{12,16},{16,20},{20,24},{24,28},{28,0},{1,5},{5... | collective-permute-start | bytes 49160 | tf_op jit(solution)/shard_map/ppermute | solution.py:25
  159.1 6.4 %collective-permute-start.13 = (bf16[64,128]{1,0:T(8,128)(2,1)S(1)}, bf16[64,128]{1,0:T(8,128)(2,1)S(1)}, u32[]{:S(2)}, u32[]{:S(2)}) collective-permute-start(bf16[64,128]{1,0:T(8,128)(2,1)S(1)} %collective-permute-done.12), channel_id=1, source_target_pairs={{0,4},{4,8},{8,12},{12,16},{16,20},{20,24},{24,28},{28,0},{1,5},{5... | collective-permute-start | bytes 49160 | tf_op jit(solution)/shard_map/ppermute | solution.py:25
  167.1 39.1 %reduce-scatter.15.cloned.1.call-start = ((), (), s32[]{:S(2)}) async-start(), calls=%async_computation.9 | async-start | bytes 327680
Sparse Core Ops, SparseCore 0:
  57.0 17.4 reduce-scatter.8
  77.1 20.0 reduce-scatter.12
  167.3 16.3 reduce-scatter.10
  186.1 20.0 reduce-scatter.14
